TPU v7x, 512 devices: a whole 4x8x8 slice. The times are simulated.
512 devices in a mesh: dp: 32 (over y, x), section: 4 (over z_hi), space: 4 (over z_lo, core).
Axes of the slice: x: 4, y: 8, z: 8 (z_hi: 4, z_lo: 2; z = z_hi * 2 + z_lo), core: 2. Of those that a mesh axis runs over, the one named last changes fastest.
Arguments:
- images: bfloat16 [64, 4, 64, 256], P('dp', 'space'), may hold values from -6 to 6
- steps: int32 [64], P('dp'), may hold values from 0 to 999
- out_grad: bfloat16 [64, 4, 64, 256], P('dp', 'space'), may hold values from -0.125 to 0.125
- conv_weight: bfloat16 [4, 3, 3, 256, 256], P('section'), may hold values from -0.125 to 0.125
- gn_gain: float32 [4, 256], P('section'), may hold values from 0.5 to 2
- emb_weight: bfloat16 [4, 256, 512], P('section'), may hold values from -0.375 to 0.375
Outputs:
- grad_conv: float32 [4, 3, 3, 256, 256], P('section')
- grad_gain: float32 [4, 256], P('section')
- grad_emb: float32 [4, 256, 512], P('section')
All inputs are finite; a program needn't handle non-finite values.
Results may differ from a plain program's by a relative error of at most 0.0064.
Values may be sent and summed in bfloat16 or wider, within the bound.
No kernel may reach another device: no remote copies, remote signals or barrier semaphores. Data moves between devices by JAX's collectives and lax.ppermute only.
A program may use at most 64 MiB of HBM per device.

v0:
```python
import math
import jax
import jax.numpy as jnp
from jax import lax
from jax.sharding import Mesh, PartitionSpec as P

G = 32
FREQ = 256
MICRO = 2
EPS = 1e-05


def from_behind(value, axis, steps):
    count = lax.axis_size(axis)
    initial, last = (max(0, -steps), min(count, count - steps))
    return lax.ppermute(value, axis, [(source, source + steps) for source in range(initial, last)])


def extended(shard, sides, width):
    for axis, dim in sides:
        size, length = (lax.axis_size(axis), shard.shape[dim])
        up = [(i, (i + 1) % size) for i in range(size - 1)]
        down = [(j, i) for i, j in up]
        last = lax.slice_in_dim(shard, length - width, length, axis=dim)
        initial = lax.slice_in_dim(shard, 0, width, axis=dim)
        before = lax.ppermute(last, axis, up)
        after = lax.ppermute(initial, axis, down)
        shard = jnp.concatenate([before, shard, after], axis=dim)
    return shard


def sinusoid(timesteps, feature_n):
    half_n = feature_n // 2
    freqs = jnp.exp(-math.log(10000.0) * jnp.arange(half_n, dtype=jnp.float32) / half_n)
    angles = timesteps.astype(jnp.float32)[:, None] * freqs[None, :]
    return jnp.concatenate([jnp.cos(angles), jnp.sin(angles)], axis=1)


def group_sums(tensor, groups):
    batch_n, height_n, width_n, channels = tensor.shape
    split = tensor.reshape(batch_n, height_n, width_n, groups, channels // groups)
    return (jnp.sum(split, axis=(1, 2, 4)), jnp.sum(split * split, axis=(1, 2, 4)))


def spread(values, channels):
    return jnp.repeat(values, channels // values.shape[1], axis=1)[:, None, None, :]


def normalize(tensor, first_sum, square_sum, gains, scales, shifts, cell_count):
    channels = tensor.shape[3]
    average = first_sum / cell_count
    inverse = lax.rsqrt(square_sum / cell_count - average * average + EPS)
    normed = (tensor - spread(average, channels)) * spread(inverse, channels) * gains
    return normed * (1.0 + scales[:, None, None, :]) + shifts[:, None, None, :]


def patches(padded, height_n, width_n):
    return jnp.concatenate(
        [
            padded[:, vertical : vertical + height_n, lateral : lateral + width_n, :]
            for vertical in range(3)
            for lateral in range(3)
        ],
        axis=3,
    )


def convolve(padded, matrix):
    batch_n, height_p, width_p, channels = padded.shape
    flat = patches(padded, height_p - 2, width_p - 2).reshape(-1, 9 * channels)
    return jnp.dot(flat, matrix, preferred_element_type=jnp.float32).reshape(
        batch_n, height_p - 2, width_p - 2, matrix.shape[1]
    )


def flip_weight(weight):
    channels = weight.shape[2]
    return jnp.transpose(weight[::-1, ::-1], (0, 1, 3, 2)).reshape(9 * channels, channels)


def silu_slope(pre_act):
    sigmoid_v = jax.nn.sigmoid(pre_act)
    return sigmoid_v * (1.0 + pre_act * (1.0 - sigmoid_v))


def pad_columns(tensor):
    return jnp.pad(tensor, ((0, 0), (0, 0), (1, 1), (0, 0)))


def pick(stacked, index):
    return lax.dynamic_index_in_dim(stacked, index, 0, keepdims=False)


def norm_backward(tensor, first_sum, square_sum, gains, scales, shifts, cell_count, d_pre):

    def mapping(tensor_v, first_v, square_v, gains_v, scales_v, shifts_v):
        return normalize(tensor_v, first_v, square_v, gains_v, scales_v, shifts_v, cell_count)

    _, pull_back = jax.vjp(mapping, tensor, first_sum, square_sum, gains, scales, shifts)
    return pull_back(d_pre)


def pad_both(tensor):
    return jnp.pad(tensor, ((0, 0), (1, 1), (1, 1), (0, 0)))


def block_forward(inputs, flat_weight, gains, scales, shifts, cell_count):
    tensor = inputs.astype(jnp.float32)
    first_sum, square_sum = group_sums(tensor, G)
    pre_act = normalize(tensor, first_sum, square_sum, gains, scales, shifts, cell_count)
    activation = jax.nn.silu(pre_act).astype(jnp.bfloat16)
    padded = pad_both(activation)
    output = (tensor + convolve(padded, flat_weight)).astype(jnp.bfloat16)
    return (output, (first_sum, square_sum, padded))


def block_backward(upstream, inputs, saved, flipped, gains, scales, shifts, cell_count):
    first_sum, square_sum, _ = saved
    channels = inputs.shape[3]
    tensor = inputs.astype(jnp.float32)
    pre_act = normalize(tensor, first_sum, square_sum, gains, scales, shifts, cell_count)
    d_act = convolve(pad_both(upstream), flipped)
    d_pre = d_act * silu_slope(pre_act)
    d_tensor, d_first, d_square, d_gains, d_scales, d_shifts = norm_backward(
        tensor, first_sum, square_sum, gains, scales, shifts, cell_count, d_pre
    )
    d_tensor = d_tensor + spread(d_first, channels) + 2.0 * tensor * spread(d_square, channels)
    d_input = (upstream.astype(jnp.float32) + d_tensor).astype(jnp.bfloat16)
    return (d_input, (d_gains, d_scales, d_shifts))


def keep(flag, new, old):
    return jax.tree.map(lambda a, b: jnp.where(flag, a, b), new, old)


def per_device(images, steps, out_grad, conv_weight, gn_gain, emb_weight):
    section_count = lax.axis_size("section")
    section_no = lax.axis_index("section")
    images = lax.all_gather(images, "space", axis=1, tiled=True)
    out_grad = lax.all_gather(out_grad, "space", axis=1, tiled=True)
    row_count = images.shape[1]
    col_count = images.shape[2]
    channels = images.shape[3]
    cell_count = row_count * col_count * (channels // G)
    weight = conv_weight[0]
    flat_weight = weight.reshape(9 * channels, channels)
    flipped = flip_weight(weight)
    gains = gn_gain[0]
    features = sinusoid(steps, FREQ)
    embedded = jnp.dot(features, emb_weight[0].astype(jnp.float32), precision=lax.Precision.HIGHEST)
    scales = embedded[:, :channels]
    shifts = embedded[:, channels:]
    last = section_count - 1
    carried = images
    kept = None
    for moment in range(section_count):
        inputs = images
        if moment > 0:
            inputs = lax.ppermute(carried, "section", [(moment - 1, moment)])
        if moment == last:
            inputs = (inputs.astype(jnp.float32) + skip.astype(jnp.float32)).astype(jnp.bfloat16)
        output, saved = block_forward(inputs, flat_weight, gains, scales, shifts, cell_count)
        if moment == 0:
            skip = lax.ppermute(output, "section", [(0, last)])
        state = (inputs, saved)
        kept = state if kept is None else keep(section_no == moment, state, kept)
        carried = output
    kept_in, kept_saved = kept
    carried = out_grad
    kept = None
    for moment in range(section_count):
        active = last - moment
        upstream = out_grad
        if moment > 0:
            upstream = lax.ppermute(carried, "section", [(active + 1, active)])
        if active == 0:
            upstream = (upstream.astype(jnp.float32) + skip_grad.astype(jnp.float32)).astype(
                jnp.bfloat16
            )
        d_input, pieces = block_backward(
            upstream, kept_in, kept_saved, flipped, gains, scales, shifts, cell_count
        )
        if moment == 0:
            skip_grad = lax.ppermute(d_input, "section", [(last, 0)])
        state = (upstream, pieces)
        kept = state if kept is None else keep(section_no == active, state, kept)
        carried = d_input
    kept_up, (d_gains, d_scales, d_shifts) = kept
    space_count = lax.axis_size("space")
    space_no = lax.axis_index("space")
    patch_rows = 9 * channels // space_count
    flat_patch = patches(kept_saved[2], row_count, col_count).reshape(-1, 9 * channels)
    own_patch = lax.dynamic_slice_in_dim(flat_patch, space_no * patch_rows, patch_rows, axis=1)
    weight_grad = jnp.dot(
        own_patch.T, kept_up.reshape(-1, channels), preferred_element_type=jnp.float32
    )
    emb_rows = FREQ // space_count
    own_features = lax.dynamic_slice_in_dim(features, space_no * emb_rows, emb_rows, axis=1)
    emb_grad = jnp.dot(
        own_features.T,
        jnp.concatenate([d_scales, d_shifts], axis=1),
        precision=lax.Precision.HIGHEST,
    )
    return reduce_grads(weight_grad, d_gains, emb_grad)


def reduce_grads(weight_grad, gain_grad, emb_grad):
    channels = gain_grad.shape[0]
    parts = [weight_grad, emb_grad.reshape(-1, channels), gain_grad[None]]
    rows = sum((part.shape[0] for part in parts))
    devices = lax.axis_size("dx") * lax.axis_size("dy")
    padded_rows = -(-rows // (8 * devices)) * 8 * devices
    parts.append(jnp.zeros((padded_rows - rows, channels), jnp.float32))
    flat = jnp.concatenate(parts, axis=0)
    for axis in ("dx", "dy"):
        flat = lax.psum_scatter(flat, axis, scatter_dimension=0, tiled=True)
    for axis in ("dy", "dx"):
        flat = lax.all_gather(flat, axis, axis=0, tiled=True)
    flat = lax.all_gather(flat, "space", axis=0)
    space_count = flat.shape[0]
    weight_rows = weight_grad.shape[0]
    emb_rows = emb_grad.size // channels
    conv = flat[:, :weight_rows].reshape(1, 3, 3, channels, channels)
    emb = flat[:, weight_rows : weight_rows + emb_rows].reshape(
        1, emb_grad.shape[0] * space_count, -1
    )
    gain = flat[0, weight_rows + emb_rows][None]
    return (conv, gain, emb)


def solution(mesh):
    dp_n = mesh.shape["dp"]
    dx_n = 4 if dp_n % 4 == 0 else 1
    mesh = Mesh(
        mesh.devices.reshape(dp_n // dx_n, dx_n, *mesh.devices.shape[1:]),
        ("dy", "dx", "section", "space"),
    )
    data = ("dy", "dx")
    in_specs = (
        P(data, "space", None, None),
        P(data),
        P(data, "space", None, None),
        P("section", None, None, None, None),
        P("section", None),
        P("section", None, None),
    )
    out_specs = (P("section", None, None, None, None), P("section", None), P("section", None, None))
    return jax.shard_map(
        per_device, mesh=mesh, in_specs=in_specs, out_specs=out_specs, check_vma=False
    )
```

profile of v0, /device:TPU:1, one launch (start us, length us, event | category | flops | bytes accessed | tf_op | source)
XLA Modules:
  0.0 301.1 jit_solution(14954645292781372341)
XLA Ops:
  8.3 12.7 %all_gather.18 = bf16[2,4,64,256]{3,2,1,0:T(8,128)(2,1)S(1)} all-gather(bf16[2,1,64,256]{3,2,1,0:T(8,128)(2,1)} %param.6), channel_id=1, replica_groups=mesh['dy'=8,'dx'=4,'section'=4,'space'=4] {'space'}, dimensions={1}, use_global_device_ids=true | all-gather | bytes 327680 | tf_op jit(solution)/shard_map/all_gather | solution.py:139
  22.4 0.9 multiply_convert_fusion.3
  24.6 1.5 fusion
  26.1 1.3 collective-permute-start
  27.4 4.7 %collective-permute-start.3 = (bf16[2,4,64,256]{3,2,1,0:T(8,128)(2,1)}, bf16[2,4,64,256]{3,2,1,0:T(8,128)(2,1)S(1)}, u32[]{:S(2)}, u32[]{:S(2)}) collective-permute-start(bf16[2,4,64,256]{3,2,1,0:T(8,128)(2,1)} %fusion), channel_id=1, source_target_pairs={{0,12},{1,13},{2,14},{3,15},{16,28},{17,29},{18,30},{19,31},{32,44... | collective-permute-start | bytes 786440 | tf_op jit(solution)/shard_map/ppermute | solution.py:164
  32.1 10.7 %all_gather.19 = bf16[2,4,64,256]{3,2,1,0:T(8,128)(2,1)S(1)} all-gather(bf16[2,1,64,256]{3,2,1,0:T(8,128)(2,1)S(1)} %copy-done.7), channel_id=1, replica_groups=mesh['dy'=8,'dx'=4,'section'=4,'space'=4] {'space'}, dimensions={1}, use_global_device_ids=true | all-gather | bytes 327680 | tf_op jit(solution)/shard_map/all_gather | solution.py:140
  42.8 0.8 fusion.61
  43.6 0.7 fusion.62
  44.3 0.7 fusion.63
  47.1 0.8 fusion.1
  47.9 0.7 collective-permute-start.1
  48.6 0.8 fusion.64
  49.3 0.7 constant_dynamic-update-slice_fusion.3
  50.1 0.8 fusion.65
  51.9 0.7 sub.50
  52.5 1.0 multiply_convert_fusion.1
  54.2 1.5 fusion.2
  55.6 1.3 collective-permute-start.2
  57.0 0.7 fusion.66
  57.7 1.6 copy.9
  59.3 1.1 rev.3
  60.4 0.7 fusion.67
  61.2 0.7 fusion.68
  61.9 2.3 fusion.28
  64.3 0.7 reduce_sum.441
  65.1 0.8 reduce_sum.444
  66.0 1.3 fusion.132
  68.2 3.3 %fusion.23 = (f32[2,256]{1,0:T(2,128)}, f32[256]{0:T(256)}, f32[2,256]{1,0:T(2,128)S(1)}, f32[2,256]{1,0:T(2,128)S(1)}, f32[2,256]{1,0:T(2,128)}, /*index=5*/f32[2,4,64,256]{3,2,1,0:T(8,128)S(1)}) fusion(bf16[2,4,64,256]{3,2,1,0:T(8,128)(2,1)S(1)} %select_select_fusion.1, f32[2,256]{1,0:T(2,128)S(1)} %mul.236, f32[2,256]{1,0:T(2,128)} %sub.58, ...), kind=kOutput, calls=%fused_computation.105 | convolution fusion | flops 607254272 | bytes 4343808 | tf_op jit(solution)/shard_map/dot_general | solution.py:71
  74.2 1.7 fusion.22
  75.9 1.4 reduce_sum.452
  77.2 1.4 reduce_sum.453
  78.7 1.4 reshape.213
  80.0 1.4 reduce_sum.455
  81.5 1.2 fusion.124
  82.7 0.7 broadcast_in_dim.46
  83.4 1.4 add.223
  84.8 1.4 broadcast_in_dim.47
  86.2 1.4 mul.509
  87.6 0.9 fusion.56
  88.5 0.7 collective-permute-start.5
  89.2 1.5 collective-permute-start.7
  91.2 2.4 fusion.21
  94.0 0.7 add.228
  95.5 1.2 fusion.59
  96.7 1.3 collective-permute-start.6
  98.7 1.4 broadcast_in_dim.41
  100.0 1.4 mul.228
  101.5 1.4 broadcast_in_dim.40
  102.8 1.4 sub.54
  104.9 13.3 %collective-permute-done.6 = bf16[2,4,64,256]{3,2,1,0:T(8,128)(2,1)} collective-permute-done((bf16[2,4,64,256]{3,2,1,0:T(8,128)(2,1)S(1)}, bf16[2,4,64,256]{3,2,1,0:T(8,128)(2,1)}, u32[]{:S(2)}, u32[]{:S(2)}) %collective-permute-start.6) | collective-permute-done | bytes 262176 | tf_op jit(solution)/shard_map/ppermute | solution.py:175
  118.1 1.2 select_select_fusion
  120.3 1.2 fusion.20
  122.8 1.3 copy-done.4
  124.5 1.8 fusion.17
  126.4 1.0 maximum_maximum_fusion
  127.5 36.3 %reduce-scatter.3.cloned.1.call-done = f32[192,256]{1,0:T(8,128)} async-done(((f32[768,256]{1,0:T(8,128)}), f32[192,256]{1,0:T(8,128)}) %reduce-scatter.3.cloned.1.call-update) | async-done | bytes 196624 | tf_op jit(solution)/shard_map/reduce_scatter | solution.py:216
  163.9 37.1 %reduce-scatter.5.cloned.1.call-done = f32[24,256]{1,0:T(8,128)} async-done(((f32[192,256]{1,0:T(8,128)}), f32[24,256]{1,0:T(8,128)}) %reduce-scatter.5.cloned.1.call-update) | async-done | bytes 24592 | tf_op jit(solution)/shard_map/reduce_scatter | solution.py:216
  201.0 19.2 %all_gather.20 = f32[192,256]{1,0:T(8,128)S(1)} all-gather(f32[24,256]{1,0:T(8,128)} %reduce-scatter.5.cloned.1.call-done), channel_id=1, replica_groups=mesh['dy'=8,'dx'=4,'section'=4,'space'=4] {'dy'}, dimensions={0}, use_global_device_ids=true | all-gather | bytes 221184 | tf_op jit(solution)/shard_map/all_gather | solution.py:218
  220.2 11.6 %all_gather.21 = f32[768,256]{1,0:T(8,128)} all-gather(f32[192,256]{1,0:T(8,128)S(1)} %all_gather.20), channel_id=1, replica_groups=mesh['dy'=8,'dx'=4,'section'=4,'space'=4] {'dx'}, dimensions={0}, use_global_device_ids=true | all-gather | bytes 983040 | tf_op jit(solution)/shard_map/all_gather | solution.py:218
  231.7 56.3 %all-gather.3.cloned.1.call-done = f32[3072,256]{1,0:T(8,128)} async-done(((f32[768,256]{1,0:T(8,128)}), f32[3072,256]{1,0:T(8,128)}) %all-gather.3.cloned.1.call-update) | async-done | bytes 3145744 | tf_op jit(solution)/shard_map/all_gather | solution.py:219
  288.1 3.2 %slice.298 = f32[4,576,256]{2,1,0:T(8,128)} slice(f32[4,768,256]{2,1,0:T(8,128)} %bitcast.40), slice={[0:4], [0:576], [0:256]} | slice | bytes 4718592 | tf_op jit(solution)/shard_map/slice | solution.py:223
  291.3 1.1 slice.300
  292.4 1.3 slice_bitcast_fusion
  293.6 0.9 reshape.218
  (226 shorter events, 16.2 us)
Async XLA Ops:
  7.2 1.0 copy-start
  7.2 16.4 %copy-start.6 = (f32[1,256]{1,0:T(1,128)S(1)}, f32[1,256]{1,0:T(1,128)}, u32[]{:S(2)}) copy-start(f32[1,256]{1,0:T(1,128)} %param.10) | copy-start | bytes 3076
  7.2 156.6 %reduce-scatter.3.cloned.1.call-start = ((), (), s32[]{:S(2)}) async-start(), calls=%async_computation.2 | async-start | bytes 983040 | tf_op jit(solution)/shard_map/reduce_scatter | solution.py:216
  8.0 13.1 %copy-start.15 = (f32[2,128]{1,0:T(2,128)}, f32[2,128]{1,0:T(2,128)S(1)}, u32[]{:S(2)}) copy-start(f32[2,128]{1,0:T(2,128)S(1)} %get-tuple-element.52) | copy-start | bytes 3076
  8.0 13.1 %copy-start.17 = (f32[2,128]{1,0:T(2,128)}, f32[2,128]{1,0:T(2,128)S(1)}, u32[]{:S(2)}) copy-start(f32[2,128]{1,0:T(2,128)S(1)} %get-tuple-element.53) | copy-start | bytes 3076
  21.4 2.5 copy-start.19
  21.5 0.6 copy-start.21
  23.3 1.3 copy-start.1
  24.0 8.1 %copy-start.7 = (bf16[2,1,64,256]{3,2,1,0:T(8,128)(2,1)S(1)}, bf16[2,1,64,256]{3,2,1,0:T(8,128)(2,1)}, u32[]{:S(2)}) copy-start(bf16[2,1,64,256]{3,2,1,0:T(8,128)(2,1)} %param.8) | copy-start | bytes 196612
  26.1 19.0 %collective-permute-start = (bf16[2,4,64,256]{3,2,1,0:T(8,128)(2,1)}, bf16[2,4,64,256]{3,2,1,0:T(8,128)(2,1)S(1)}, u32[]{:S(2)}, u32[]{:S(2)}) collective-permute-start(bf16[2,4,64,256]{3,2,1,0:T(8,128)(2,1)} %fusion), channel_id=1, source_target_pairs={{0,4},{1,5},{2,6},{3,7},{16,20},{17,21},{18,22},{19,23},{32,36},{3... | collective-permute-start | bytes 786440 | tf_op jit(solution)/shard_map/ppermute | solution.py:159
  27.4 34.5 %collective-permute-start.3 = (bf16[2,4,64,256]{3,2,1,0:T(8,128)(2,1)}, bf16[2,4,64,256]{3,2,1,0:T(8,128)(2,1)S(1)}, u32[]{:S(2)}, u32[]{:S(2)}) collective-permute-start(bf16[2,4,64,256]{3,2,1,0:T(8,128)(2,1)} %fusion), channel_id=1, source_target_pairs={{0,12},{1,13},{2,14},{3,15},{16,28},{17,29},{18,30},{19,31},{32,44... | collective-permute-start | bytes 786440 | tf_op jit(solution)/shard_map/ppermute | solution.py:164
  45.3 0.6 copy-start.22
  45.5 0.6 copy-start.23
  47.9 2.9 collective-permute-start.1
  51.1 0.6 copy-start.24
  51.3 0.6 copy-start.25
  52.5 1.2 copy-start.11
  55.6 6.3 %collective-permute-start.2 = (bf16[2,4,64,256]{3,2,1,0:T(8,128)(2,1)}, bf16[2,4,64,256]{3,2,1,0:T(8,128)(2,1)}, u32[]{:S(2)}, u32[]{:S(2)}) collective-permute-start(bf16[2,4,64,256]{3,2,1,0:T(8,128)(2,1)} %fusion.2), channel_id=1, source_target_pairs={{8,12},{9,13},{10,14},{11,15},{24,28},{25,29},{26,30},{27,31},{40,... | collective-permute-start | bytes 786440 | tf_op jit(solution)/shard_map/ppermute | solution.py:159
  59.3 6.6 %copy-start.20 = (f32[2,32]{1,0:T(2,128)S(1)}, f32[2,32]{1,0:T(2,128)}, u32[]{:S(2)}) copy-start(f32[2,32]{1,0:T(2,128)} %copy-done.19) | copy-start | bytes 772
  60.4 7.8 %copy-start.2 = (bf16[3,3,256,256]{2,3,1,0:T(8,128)(2,1)S(1)}, bf16[3,3,256,256]{2,3,1,0:T(8,128)(2,1)}, u32[]{:S(2)}) copy-start(bf16[3,3,256,256]{2,3,1,0:T(8,128)(2,1)} %rev.3) | copy-start | bytes 3538948
  67.2 0.9 copy-start.8
  68.2 3.7 %copy-start.9 = (f32[2,32]{1,0:T(2,128)S(1)}, f32[2,32]{1,0:T(2,128)}, u32[]{:S(2)}) copy-start(f32[2,32]{1,0:T(2,128)} %copy-done.8) | copy-start | bytes 772
  68.2 3.7 %copy-start.26 = (f32[2,32]{1,0:T(2,128)S(1)}, f32[2,32]{1,0:T(2,128)}, u32[]{:S(2)}) copy-start(f32[2,32]{1,0:T(2,128)} %get-tuple-element.34) | copy-start | bytes 772
  72.0 0.5 copy-start.13
  73.0 1.1 copy-start.5
  73.0 1.2 copy-start.27
  73.0 0.7 collective-permute-start.4
  88.5 2.6 copy-start.28
  88.5 2.2 collective-permute-start.5
  89.2 15.7 %collective-permute-start.7 = (bf16[2,4,64,256]{3,2,1,0:T(8,128)(2,1)}, bf16[2,4,64,256]{3,2,1,0:T(8,128)(2,1)}, u32[]{:S(2)}, u32[]{:S(2)}) collective-permute-start(bf16[2,4,64,256]{3,2,1,0:T(8,128)(2,1)} %copy-done.5), channel_id=1, source_target_pairs={{12,0},{13,1},{14,2},{15,3},{28,16},{29,17},{30,18},{31,19},{44,32... | collective-permute-start | bytes 786440 | tf_op jit(solution)/shard_map/ppermute | solution.py:184
  91.1 2.8 copy-start.10
  91.1 2.8 copy-start.14
  96.7 21.4 %collective-permute-start.6 = (bf16[2,4,64,256]{3,2,1,0:T(8,128)(2,1)S(1)}, bf16[2,4,64,256]{3,2,1,0:T(8,128)(2,1)}, u32[]{:S(2)}, u32[]{:S(2)}) collective-permute-start(bf16[2,4,64,256]{3,2,1,0:T(8,128)(2,1)S(1)} %fusion.59), channel_id=1, source_target_pairs={{4,0},{5,1},{6,2},{7,3},{20,16},{21,17},{22,18},{23,19},{36,32},{3... | collective-permute-start | bytes 786440 | tf_op jit(solution)/shard_map/ppermute | solution.py:175
  119.4 1.0 copy-start.3
  119.4 0.9 copy-start.29
  119.4 0.9 copy-start.30
  119.4 0.9 copy-start.31
  122.0 0.7 copy-start.32
  122.0 0.7 copy-start.33
  122.0 0.7 copy-start.34
  122.1 0.7 copy-start.35
  122.1 0.7 copy-start.36
  122.1 0.7 copy-start.37
  122.1 2.0 copy-start.16
  122.1 2.0 copy-start.18
  122.3 4.0 %copy-start.38 = (f32[256]{0:T(256)S(1)}, f32[256]{0:T(256)}, u32[]{:S(2)}) copy-start(f32[256]{0:T(256)} %get-tuple-element.4) | copy-start | bytes 3076
  122.3 4.0 %copy-start.39 = (f32[256]{0:T(256)S(1)}, f32[256]{0:T(256)}, u32[]{:S(2)}) copy-start(f32[256]{0:T(256)} %get-tuple-element.7) | copy-start | bytes 3076
  122.3 4.0 %copy-start.40 = (f32[256]{0:T(256)S(1)}, f32[256]{0:T(256)}, u32[]{:S(2)}) copy-start(f32[256]{0:T(256)} %get-tuple-element.10) | copy-start | bytes 3076
  122.3 4.0 %copy-start.12 = (f32[768]{0:T(1024)S(1)}, f32[768]{0:T(1024)}, u32[]{:S(2)}) copy-start(f32[768]{0:T(1024)} %pad.36.clone) | copy-start | bytes 9220
  122.7 1.4 copy-start.4
  127.4 73.5 %reduce-scatter.5.cloned.1.call-start = ((), (), s32[]{:S(2)}) async-start(), calls=%async_computation.3 | async-start | bytes 221184 | tf_op jit(solution)/shard_map/reduce_scatter | solution.py:216
  163.8 124.2 %all-gather.3.cloned.1.call-start = ((), (), s32[]{:S(2)}) async-start(), calls=%async_computation.4 | async-start | bytes 3932160 | tf_op jit(solution)/shard_map/all_gather | solution.py:219
Sparse Core Ops, SparseCore 0:
  127.6 36.1 reduce-scatter.2
  166.6 34.3 reduce-scatter.4
  231.9 56.1 all-gather.2
where the time goes:
time: 302 us; the launch traced here: 301 us
  waiting for transfers between devices  144 us (48%)
  blocking collectives  54.2 us (18%)
  local copies, waits for them, and re-layouts  43.6 us (14%)
  other arithmetic  17.7 us (6%)
  between operations  15 us (5%)
  matrix products  14.7 us (5%)
  starting transfers between devices  12.2 us (4%)
    reduce_scatter x2, waiting for transfers between devices, reduce_grads(): flat = lax.psum_scatter(flat, axis, scatter_dimension=0, tiled=True)  73.4 us
    all_gather x1, waiting for transfers between devices, reduce_grads(): flat = lax.all_gather(flat, 'space', axis=0)  56.3 us
    all_gather x2, blocking collectives, reduce_grads(): flat = lax.all_gather(flat, axis, axis=0, tiled=True)  30.7 us
    unnamed x144, local copies, waits for them, and re-layouts  14.3 us
    ppermute x3, waiting for transfers between devices, per_device(): upstream = lax.ppermute(carried, 'section', [(active + 1, active)])  13.3 us
    all_gather x1, blocking collectives, per_device(): images = lax.all_gather(images, 'space', axis=1, tiled=True)  12.7 us
    dot_general x7, matrix products, convolve(): jnp.dot(flat, matrix, preferred_element_type=jnp.float32)  12.3 us
    all_gather x1, blocking collectives, per_device(): out_grad = lax.all_gather(out_grad, 'space', axis=1, tiled=True)  10.7 us
  transfers between devices with their start and end apart: 11, of which 5 were waited for; matrix products, arithmetic and copies ran while one was open for 9% of the time, Pallas kernels for 0%

commit v1 on v0

--- a/solution.py
+++ b/solution.py
@@ -136,7 +136,9 @@
 def per_device(images, steps, out_grad, conv_weight, gn_gain, emb_weight):
     section_count = lax.axis_size("section")
     section_no = lax.axis_index("section")
-    images = lax.all_gather(images, "space", axis=1, tiled=True)
+    images = jnp.concatenate(
+        lax.all_to_all(jnp.stack([images] * lax.axis_size("space")), "space", 0, 0), axis=1
+    )
     out_grad = lax.all_gather(out_grad, "space", axis=1, tiled=True)
     row_count = images.shape[1]
     col_count = images.shape[2]

time: 302 us -> 305 us (level)
  blocking collectives: 54.2 us -> 38.2 us
  waiting for transfers between devices: 144 us -> 153 us
  starting transfers between devices: 12.2 us -> 19.1 us
    all_gather x1 -> x0, blocking collectives: 12.7 us -> none  [per_device(): images = lax.all_gather(images, 'space', axis=1, tiled=True)]
    all_to_all x0 -> x1, starting transfers between devices: none -> 10.3 us  [per_device(): lax.all_to_all(jnp.stack([images] * lax.axis_size('space')), 'space', 0, 0)]
    ppermute x1, waiting for transfers between devices: 0.65 us -> 5.57 us  [per_device(): skip_grad = lax.ppermute(d_input, 'section', [(last, 0)])]
    ppermute x3, waiting for transfers between devices: 0.01 us -> 3.89 us  [per_device(): inputs = lax.ppermute(carried, 'section', [(moment - 1, moment)])]
    ppermute x1, starting transfers between devices: 4.67 us -> 1.29 us  [per_device(): skip = lax.ppermute(output, 'section', [(0, last)])]
    all_gather x1, blocking collectives: 10.7 us -> 7.45 us  [per_device(): out_grad = lax.all_gather(out_grad, 'space', axis=1, tiled=True)]
  transfers between devices with their start and end apart: 11 -> 12, of which waited for: 5 -> 6; matrix products, arithmetic and copies ran while one was open for 9% -> 9% of each run, Pallas kernels for 0% -> 0%
where the time goes in v1:
time: 305 us; the launch traced here: 304 us
  waiting for transfers between devices  153 us (50%)
  local copies, waits for them, and re-layouts  45.3 us (15%)
  blocking collectives  38.2 us (13%)
  starting transfers between devices  19.1 us (6%)
  other arithmetic  17.7 us (6%)
  matrix products  15.3 us (5%)
  between operations  15 us (5%)
    reduce_scatter x2, waiting for transfers between devices, reduce_grads(): flat = lax.psum_scatter(flat, axis, scatter_dimension=0, tiled=True)  74.1 us
    all_gather x1, waiting for transfers between devices, reduce_grads(): flat = lax.all_gather(flat, 'space', axis=0)  56.4 us
    all_gather x2, blocking collectives, reduce_grads(): flat = lax.all_gather(flat, axis, axis=0, tiled=True)  30.8 us
    unnamed x144, local copies, waits for them, and re-layouts  14.4 us
    ppermute x3, waiting for transfers between devices, per_device(): upstream = lax.ppermute(carried, 'section', [(active + 1, active)])  13.3 us
    dot_general x7, matrix products, convolve(): jnp.dot(flat, matrix, preferred_element_type=jnp.float32)  12.9 us
    all_to_all x1, starting transfers between devices, per_device(): lax.all_to_all(jnp.stack([images] * lax.axis_size('space')), 'space', 0, 0)  10.3 us
    all_gather x1, blocking collectives, per_device(): out_grad = lax.all_gather(out_grad, 'space', axis=1, tiled=True)  7.45 us
  transfers between devices with their start and end apart: 12, of which 6 were waited for; matrix products, arithmetic and copies ran while one was open for 9% of the time, Pallas kernels for 0%

profile of v1, /device:TPU:1, one launch (start us, length us, event | category | flops | bytes accessed | tf_op | source)
XLA Modules:
  0.0 303.9 jit_solution(2340435281770882576)
XLA Ops:
  7.2 1.6 stack.2
  8.8 10.3 %all-to-all-start = ((bf16[4,2,1,64,256]{4,3,1,2,0:T(8,128)(2,1)}), bf16[4,2,1,64,256]{4,3,1,2,0:T(8,128)(2,1)S(1)}, u32[]{:S(2)}, u32[]{:S(2)}) async-start(bf16[4,2,1,64,256]{4,3,1,2,0:T(8,128)(2,1)} %stack.2), calls=%async_computation | async-start | bytes 524288 | tf_op jit(solution)/shard_map/all_to_all | solution.py:140
  19.7 7.5 %all_gather.15 = bf16[2,4,64,256]{3,2,1,0:T(8,128)(2,1)S(1)} all-gather(bf16[2,1,64,256]{3,2,1,0:T(8,128)(2,1)} %param.8), channel_id=1, replica_groups=mesh['dy'=8,'dx'=4,'section'=4,'space'=4] {'space'}, dimensions={1}, use_global_device_ids=true | all-gather | bytes 327680 | tf_op jit(solution)/shard_map/all_gather | solution.py:142
  29.2 0.9 multiply_convert_fusion.3
  31.3 1.5 fusion
  32.8 1.3 collective-permute-start
  34.1 0.8 fusion.61
  34.9 0.7 fusion.62
  35.6 0.7 fusion.63
  36.3 3.9 %collective-permute-done = bf16[2,4,64,256]{3,2,1,0:T(8,128)(2,1)S(1)} collective-permute-done((bf16[2,4,64,256]{3,2,1,0:T(8,128)(2,1)}, bf16[2,4,64,256]{3,2,1,0:T(8,128)(2,1)S(1)}, u32[]{:S(2)}, u32[]{:S(2)}) %collective-permute-start) | collective-permute-done | bytes 262176 | tf_op jit(solution)/shard_map/ppermute | solution.py:161
  42.3 0.8 fusion.1
  43.8 0.8 fusion.64
  44.5 0.7 constant_dynamic-update-slice_fusion.3
  45.3 0.8 fusion.65
  46.0 1.3 collective-permute-start.3
  48.4 0.7 sub.50
  49.1 1.0 multiply_convert_fusion.1
  50.7 1.5 fusion.2
  52.2 1.3 collective-permute-start.2
  53.5 0.7 fusion.66
  54.3 1.6 copy.11
  55.8 1.1 rev.3
  56.9 0.7 fusion.67
  57.7 0.7 fusion.68
  58.4 2.3 fusion.33
  60.8 0.7 reduce_sum.441
  61.6 0.8 reduce_sum.444
  62.5 1.3 fusion.134
  64.7 3.3 %fusion.28 = (f32[2,256]{1,0:T(2,128)}, f32[256]{0:T(256)}, f32[2,256]{1,0:T(2,128)S(1)}, f32[2,256]{1,0:T(2,128)S(1)}, f32[2,256]{1,0:T(2,128)}, /*index=5*/f32[2,4,64,256]{3,2,1,0:T(8,128)S(1)}) fusion(bf16[2,4,64,256]{3,2,1,0:T(8,128)(2,1)S(1)} %fusion.118, f32[2,256]{1,0:T(2,128)S(1)} %mul.236, f32[2,256]{1,0:T(2,128)} %sub.58, f32[256]{0:T(256)S(1)} %bitcast.74, ...), kind=kOutput, calls=%fused_computation.110 | convolution fusion | flops 607254272 | bytes 4343808 | tf_op jit(solution)/shard_map/dot_general | solution.py:71
  70.7 1.7 fusion.27
  72.4 1.4 reduce_sum.452
  73.7 1.4 reduce_sum.453
  75.2 1.4 reshape.225
  76.5 1.4 reduce_sum.455
  78.0 1.2 fusion.126
  79.2 0.7 broadcast_in_dim.46
  79.9 1.4 add.223
  81.3 1.4 broadcast_in_dim.47
  82.7 1.4 mul.509
  84.1 0.9 fusion.56
  85.7 1.5 collective-permute-start.7
  87.7 2.4 fusion.26
  92.0 1.2 fusion.59
  93.2 1.3 collective-permute-start.6
  95.2 1.4 broadcast_in_dim.41
  96.5 1.4 mul.228
  98.0 1.4 broadcast_in_dim.40
  99.3 1.4 sub.54
  100.7 5.6 %collective-permute-done.7 = bf16[2,4,64,256]{3,2,1,0:T(8,128)(2,1)} collective-permute-done((bf16[2,4,64,256]{3,2,1,0:T(8,128)(2,1)}, bf16[2,4,64,256]{3,2,1,0:T(8,128)(2,1)}, u32[]{:S(2)}, u32[]{:S(2)}) %collective-permute-start.7) | collective-permute-done | bytes 262176 | tf_op jit(solution)/shard_map/ppermute | solution.py:186
  106.3 13.3 %collective-permute-done.6 = bf16[2,4,64,256]{3,2,1,0:T(8,128)(2,1)} collective-permute-done((bf16[2,4,64,256]{3,2,1,0:T(8,128)(2,1)S(1)}, bf16[2,4,64,256]{3,2,1,0:T(8,128)(2,1)}, u32[]{:S(2)}, u32[]{:S(2)}) %collective-permute-start.6) | collective-permute-done | bytes 262176 | tf_op jit(solution)/shard_map/ppermute | solution.py:177
  119.5 1.2 select_select_fusion
  121.7 1.7 fusion.25
  124.8 1.3 copy-done.4
  126.5 1.8 fusion.17
  128.4 1.0 maximum_maximum_fusion
  129.5 37.0 %reduce-scatter.3.cloned.1.call-done = f32[192,256]{1,0:T(8,128)} async-done(((f32[768,256]{1,0:T(8,128)}), f32[192,256]{1,0:T(8,128)}) %reduce-scatter.3.cloned.1.call-update) | async-done | bytes 196624 | tf_op jit(solution)/shard_map/reduce_scatter | solution.py:218
  166.6 37.1 %reduce-scatter.5.cloned.1.call-done = f32[24,256]{1,0:T(8,128)} async-done(((f32[192,256]{1,0:T(8,128)}), f32[24,256]{1,0:T(8,128)}) %reduce-scatter.5.cloned.1.call-update) | async-done | bytes 24592 | tf_op jit(solution)/shard_map/reduce_scatter | solution.py:218
  203.7 19.2 %all_gather.16 = f32[192,256]{1,0:T(8,128)S(1)} all-gather(f32[24,256]{1,0:T(8,128)} %reduce-scatter.5.cloned.1.call-done), channel_id=1, replica_groups=mesh['dy'=8,'dx'=4,'section'=4,'space'=4] {'dy'}, dimensions={0}, use_global_device_ids=true | all-gather | bytes 221184 | tf_op jit(solution)/shard_map/all_gather | solution.py:220
  222.8 11.6 %all_gather.17 = f32[768,256]{1,0:T(8,128)} all-gather(f32[192,256]{1,0:T(8,128)S(1)} %all_gather.16), channel_id=1, replica_groups=mesh['dy'=8,'dx'=4,'section'=4,'space'=4] {'dx'}, dimensions={0}, use_global_device_ids=true | all-gather | bytes 983040 | tf_op jit(solution)/shard_map/all_gather | solution.py:220
  234.5 56.4 %all-gather.3.cloned.1.call-done = f32[3072,256]{1,0:T(8,128)} async-done(((f32[768,256]{1,0:T(8,128)}), f32[3072,256]{1,0:T(8,128)}) %all-gather.3.cloned.1.call-update) | async-done | bytes 3145744 | tf_op jit(solution)/shard_map/all_gather | solution.py:221
  290.9 3.2 %slice.298 = f32[4,576,256]{2,1,0:T(8,128)} slice(f32[4,768,256]{2,1,0:T(8,128)} %bitcast.55), slice={[0:4], [0:576], [0:256]} | slice | bytes 4718592 | tf_op jit(solution)/shard_map/slice | solution.py:225
  294.1 1.1 slice.300
  295.2 1.3 slice_bitcast_fusion
  296.4 0.9 reshape.230
  (228 shorter events, 17.7 us)
Async XLA Ops:
  7.2 20.1 %copy-start = (bf16[1,256,512]{2,1,0:T(8,128)(2,1)S(1)}, bf16[1,256,512]{2,1,0:T(8,128)(2,1)}, u32[]{:S(2)}) copy-start(bf16[1,256,512]{2,1,0:T(8,128)(2,1)} %param.11) | copy-start | bytes 786436
  7.2 23.1 %copy-start.6 = (f32[1,256]{1,0:T(1,128)S(1)}, f32[1,256]{1,0:T(1,128)}, u32[]{:S(2)}) copy-start(f32[1,256]{1,0:T(1,128)} %param.10) | copy-start | bytes 3076
  8.8 18.7 %all-to-all-start = ((bf16[4,2,1,64,256]{4,3,1,2,0:T(8,128)(2,1)}), bf16[4,2,1,64,256]{4,3,1,2,0:T(8,128)(2,1)S(1)}, u32[]{:S(2)}, u32[]{:S(2)}) async-start(bf16[4,2,1,64,256]{4,3,1,2,0:T(8,128)(2,1)} %stack.2), calls=%async_computation | async-start | bytes 524288 | tf_op jit(solution)/shard_map/all_to_all | solution.py:140
  19.0 147.5 %reduce-scatter.3.cloned.1.call-start = ((), (), s32[]{:S(2)}) async-start(), calls=%async_computation.3 | async-start | bytes 983040 | tf_op jit(solution)/shard_map/reduce_scatter | solution.py:218
  27.3 0.6 copy-start.14
  27.3 0.6 copy-start.16
  28.1 1.0 copy-start.18
  28.2 0.6 copy-start.20
  30.1 1.3 copy-start.1
  32.8 7.4 %collective-permute-start = (bf16[2,4,64,256]{3,2,1,0:T(8,128)(2,1)}, bf16[2,4,64,256]{3,2,1,0:T(8,128)(2,1)S(1)}, u32[]{:S(2)}, u32[]{:S(2)}) collective-permute-start(bf16[2,4,64,256]{3,2,1,0:T(8,128)(2,1)} %fusion), channel_id=1, source_target_pairs={{0,4},{1,5},{2,6},{3,7},{16,20},{17,21},{18,22},{19,23},{32,36},{3... | collective-permute-start | bytes 786440 | tf_op jit(solution)/shard_map/ppermute | solution.py:161
  40.5 0.6 copy-start.21
  40.7 0.6 copy-start.22
  43.1 4.2 %collective-permute-start.1 = (bf16[2,4,64,256]{3,2,1,0:T(8,128)(2,1)S(1)}, bf16[2,4,64,256]{3,2,1,0:T(8,128)(2,1)S(1)}, u32[]{:S(2)}, u32[]{:S(2)}) collective-permute-start(bf16[2,4,64,256]{3,2,1,0:T(8,128)(2,1)S(1)} %fusion.1), channel_id=1, source_target_pairs={{4,8},{5,9},{6,10},{7,11},{20,24},{21,25},{22,26},{23,27},{36,40},... | collective-permute-start | bytes 786440 | tf_op jit(solution)/shard_map/ppermute | solution.py:161
  46.0 12.4 %collective-permute-start.3 = (bf16[2,4,64,256]{3,2,1,0:T(8,128)(2,1)}, bf16[2,4,64,256]{3,2,1,0:T(8,128)(2,1)S(1)}, u32[]{:S(2)}, u32[]{:S(2)}) collective-permute-start(bf16[2,4,64,256]{3,2,1,0:T(8,128)(2,1)} %fusion), channel_id=1, source_target_pairs={{0,12},{1,13},{2,14},{3,15},{16,28},{17,29},{18,30},{19,31},{32,44... | collective-permute-start | bytes 786440 | tf_op jit(solution)/shard_map/ppermute | solution.py:166
  47.6 0.6 copy-start.23
  47.8 0.6 copy-start.24
  49.1 1.2 copy-start.10
  52.2 6.3 %collective-permute-start.2 = (bf16[2,4,64,256]{3,2,1,0:T(8,128)(2,1)}, bf16[2,4,64,256]{3,2,1,0:T(8,128)(2,1)}, u32[]{:S(2)}, u32[]{:S(2)}) collective-permute-start(bf16[2,4,64,256]{3,2,1,0:T(8,128)(2,1)} %fusion.2), channel_id=1, source_target_pairs={{8,12},{9,13},{10,14},{11,15},{24,28},{25,29},{26,30},{27,31},{40,... | collective-permute-start | bytes 786440 | tf_op jit(solution)/shard_map/ppermute | solution.py:161
  55.8 6.6 %copy-start.19 = (f32[2,32]{1,0:T(2,128)S(1)}, f32[2,32]{1,0:T(2,128)}, u32[]{:S(2)}) copy-start(f32[2,32]{1,0:T(2,128)} %copy-done.18) | copy-start | bytes 772
  56.9 7.8 %copy-start.2 = (bf16[3,3,256,256]{2,3,1,0:T(8,128)(2,1)S(1)}, bf16[3,3,256,256]{2,3,1,0:T(8,128)(2,1)}, u32[]{:S(2)}) copy-start(bf16[3,3,256,256]{2,3,1,0:T(8,128)(2,1)} %rev.3) | copy-start | bytes 3538948
  63.7 0.9 copy-start.7
  64.7 3.7 %copy-start.8 = (f32[2,32]{1,0:T(2,128)S(1)}, f32[2,32]{1,0:T(2,128)}, u32[]{:S(2)}) copy-start(f32[2,32]{1,0:T(2,128)} %copy-done.7) | copy-start | bytes 772
  64.7 3.7 %copy-start.25 = (f32[2,32]{1,0:T(2,128)S(1)}, f32[2,32]{1,0:T(2,128)}, u32[]{:S(2)}) copy-start(f32[2,32]{1,0:T(2,128)} %get-tuple-element.34) | copy-start | bytes 772
  68.5 0.5 copy-start.12
  69.5 1.1 copy-start.5
  69.5 1.2 copy-start.26
  69.5 0.7 collective-permute-start.4
  85.0 2.6 copy-start.27
  85.0 2.2 collective-permute-start.5
  85.7 20.6 %collective-permute-start.7 = (bf16[2,4,64,256]{3,2,1,0:T(8,128)(2,1)}, bf16[2,4,64,256]{3,2,1,0:T(8,128)(2,1)}, u32[]{:S(2)}, u32[]{:S(2)}) collective-permute-start(bf16[2,4,64,256]{3,2,1,0:T(8,128)(2,1)} %copy-done.5), channel_id=1, source_target_pairs={{12,0},{13,1},{14,2},{15,3},{28,16},{29,17},{30,18},{31,19},{44,32... | collective-permute-start | bytes 786440 | tf_op jit(solution)/shard_map/ppermute | solution.py:186
  87.6 2.8 copy-start.9
  87.6 2.8 copy-start.13
  93.2 26.3 %collective-permute-start.6 = (bf16[2,4,64,256]{3,2,1,0:T(8,128)(2,1)S(1)}, bf16[2,4,64,256]{3,2,1,0:T(8,128)(2,1)}, u32[]{:S(2)}, u32[]{:S(2)}) collective-permute-start(bf16[2,4,64,256]{3,2,1,0:T(8,128)(2,1)S(1)} %fusion.59), channel_id=1, source_target_pairs={{4,0},{5,1},{6,2},{7,3},{20,16},{21,17},{22,18},{23,19},{36,32},{3... | collective-permute-start | bytes 786440 | tf_op jit(solution)/shard_map/ppermute | solution.py:177
  120.8 1.0 copy-start.3
  120.8 0.9 copy-start.28
  120.8 0.9 copy-start.29
  120.8 0.9 copy-start.30
  124.0 0.7 copy-start.31
  124.0 0.7 copy-start.32
  124.0 0.7 copy-start.33
  124.0 0.7 copy-start.34
  124.0 0.7 copy-start.35
  124.1 0.7 copy-start.36
  124.1 2.0 copy-start.15
  124.1 2.0 copy-start.17
  124.3 4.0 %copy-start.37 = (f32[256]{0:T(256)S(1)}, f32[256]{0:T(256)}, u32[]{:S(2)}) copy-start(f32[256]{0:T(256)} %get-tuple-element.4) | copy-start | bytes 3076
  124.3 4.0 %copy-start.38 = (f32[256]{0:T(256)S(1)}, f32[256]{0:T(256)}, u32[]{:S(2)}) copy-start(f32[256]{0:T(256)} %get-tuple-element.7) | copy-start | bytes 3076
  124.3 4.0 %copy-start.39 = (f32[256]{0:T(256)S(1)}, f32[256]{0:T(256)}, u32[]{:S(2)}) copy-start(f32[256]{0:T(256)} %get-tuple-element.10) | copy-start | bytes 3076
  124.3 4.0 %copy-start.40 = (f32[256]{0:T(256)S(1)}, f32[256]{0:T(256)}, u32[]{:S(2)}) copy-start(f32[256]{0:T(256)} %get-tuple-element.13) | copy-start | bytes 3076
  124.3 4.0 %copy-start.11 = (f32[768]{0:T(1024)S(1)}, f32[768]{0:T(1024)}, u32[]{:S(2)}) copy-start(f32[768]{0:T(1024)} %pad.36.clone) | copy-start | bytes 9220
  124.7 1.4 copy-start.4
  129.5 74.2 %reduce-scatter.5.cloned.1.call-start = ((), (), s32[]{:S(2)}) async-start(), calls=%async_computation.4 | async-start | bytes 221184 | tf_op jit(solution)/shard_map/reduce_scatter | solution.py:218
  166.5 124.3 %all-gather.3.cloned.1.call-start = ((), (), s32[]{:S(2)}) async-start(), calls=%async_computation.5 | async-start | bytes 3932160 | tf_op jit(solution)/shard_map/all_gather | solution.py:221
Sparse Core Ops, SparseCore 0:
  129.6 36.8 reduce-scatter.2
  169.3 34.3 reduce-scatter.4
  234.6 56.2 all-gather.2
